TPU v7x, 128 devices: a whole 4x4x4 slice. The times are simulated.
128 devices in a mesh: pipe: 2 (over core), dp: 16 (over y, x), tensor: 4 (over z).
Axes of the slice: x: 4, y: 4, z: 4, core: 2. Of those that a mesh axis runs over, the one named last changes fastest.
Arguments:
- weights: bfloat16 [2, 8192, 8192], P('pipe', 'tensor', 'dp'), may hold values from -0.0625 to 0.0625
- inputs: bfloat16 [2, 2, 32, 64, 8192], P('pipe', None, 'dp', None, 'tensor'), may hold values from -150 to 150
- cotangent: bfloat16 [2, 32, 64, 8192], P(None, 'dp', None, 'tensor'), may hold values from -6 to 6
- clip_norm: float32 [1], replicated, may hold values from 8192 to 12582912
- noise: bfloat16 [2, 8192, 8192], P('pipe', 'tensor', 'dp'), may hold values from -6 to 6
Outputs:
- grads: float32 [2, 8192, 8192], P('pipe', 'tensor', 'dp')
- clip_factors: float32 [2, 32], P(None, 'dp')
All inputs are finite; a program needn't handle non-finite values.
Results may differ from a plain program's by a relative error of at most 0.015.
Values may be sent and summed in bfloat16 or wider, within the bound.
No kernel may reach another device: no remote copies, remote signals or barrier semaphores. Data moves between devices by JAX's collectives and lax.ppermute only.
A program may use at most 128 MiB of HBM per device.

v0:
```python
import jax
import jax.numpy as jnp
from jax import lax
from jax.sharding import PartitionSpec as P


def swapped(value, axis):
    count = lax.axis_size(axis)
    return lax.ppermute(value, axis, [(source, count - 1 - source) for source in range(count)])


def to_column_blocks(values, group_count, column_part):
    micro_count, example_count, length_count, _ = values.shape
    token_count = example_count * length_count
    full = lax.all_gather(values, "tensor", axis=3, tiled=True)
    by_block = full.reshape(micro_count, token_count, group_count, column_part)
    moved = lax.all_to_all(by_block, "dp", split_axis=2, concat_axis=1, tiled=True)
    return moved.reshape(micro_count, group_count * token_count, column_part)


def grams(values):
    return lax.psum(
        jnp.einsum("...ld,...kd->...lk", values, values, preferred_element_type=jnp.float32),
        "tensor",
    )


def local(weights, inputs, cotangent, clip_norm, noise):
    section_index = lax.axis_index("pipe")
    group_count = lax.axis_size("dp")
    weight_block = weights[0]
    local_inputs = inputs[0]
    micro_count, example_count, length_count, width_part = local_inputs.shape
    token_count = example_count * length_count
    column_part = weight_block.shape[1]
    full_width = column_part * group_count
    is_last = section_index == 1
    gathered_inputs = lax.all_gather(local_inputs, "dp", axis=1, tiled=True)
    input_grams = grams(local_inputs)
    last_grams = grams(cotangent)
    last_blocks = to_column_blocks(cotangent, group_count, column_part)
    last_weights = jnp.where(is_last, weight_block, swapped(weight_block, "pipe"))
    own_blocks = lax.dynamic_index_in_dim(last_blocks, section_index, 0, keepdims=False)
    own_cotangent = lax.dynamic_index_in_dim(cotangent, section_index, 0, keepdims=False)
    terms = lax.dot_general(
        own_blocks, last_weights, (((1,), (1,)), ((), ())), preferred_element_type=jnp.float32
    ).astype(jnp.bfloat16)
    summed = lax.psum_scatter(terms, "dp", scatter_dimension=0, tiled=True).astype(jnp.float32)
    renewed = (
        (own_cotangent.reshape(token_count, width_part).astype(jnp.float32) + summed)
        .astype(jnp.bfloat16)
        .reshape(1, example_count, length_count, width_part)
    )
    own_first_grams = grams(renewed)
    other_first_grams = swapped(own_first_grams, "pipe")
    first_grams = jnp.where(
        is_last,
        jnp.concatenate([other_first_grams, own_first_grams], 0),
        jnp.concatenate([own_first_grams, other_first_grams], 0),
    )
    output_grams = jnp.where(is_last, last_grams, first_grams)
    section_terms = jnp.sum(input_grams * output_grams, axis=(2, 3))
    norm_square = lax.psum(section_terms, "pipe")
    bound = clip_norm[0]
    scale_terms = bound / jnp.maximum(jnp.sqrt(norm_square), bound)
    all_scales = lax.all_gather(scale_terms, "dp", axis=1, tiled=True)
    own_first_blocks = to_column_blocks(renewed, group_count, column_part)
    other_first_blocks = swapped(own_first_blocks, "pipe")
    first_blocks = jnp.where(
        is_last,
        jnp.concatenate([other_first_blocks, own_first_blocks], 0),
        jnp.concatenate([own_first_blocks, other_first_blocks], 0),
    )
    grad_blocks = jnp.where(is_last, last_blocks, first_blocks)
    clipped = (gathered_inputs.astype(jnp.float32) * all_scales[:, :, None, None]).astype(
        jnp.bfloat16
    )
    flat_inputs = clipped.reshape(micro_count * group_count * token_count, width_part)
    flat_grads = grad_blocks.reshape(micro_count * group_count * token_count, column_part)
    summed_grad = lax.dot_general(
        flat_inputs, flat_grads, (((0,), (0,)), ((), ())), preferred_element_type=jnp.float32
    )
    noise_weight = 1.5 / full_width
    per_example_sum = micro_count * group_count * example_count
    final_output = (
        summed_grad + noise_weight * bound * noise[0].astype(jnp.float32)
    ) / per_example_sum
    return (final_output[None], scale_terms)


def solution(mesh):
    in_specs = (
        P("pipe", "tensor", "dp"),
        P("pipe", None, "dp", None, "tensor"),
        P(None, "dp", None, "tensor"),
        P(),
        P("pipe", "tensor", "dp"),
    )
    out_specs = (P("pipe", "tensor", "dp"), P(None, "dp"))
    return jax.shard_map(local, mesh=mesh, in_specs=in_specs, out_specs=out_specs, check_vma=False)
```

profile of v0, /device:TPU:1, one launch (start us, length us, event | category | flops | bytes accessed | tf_op | source)
XLA Modules:
  0.0 456.7 jit_solution(14960222356371423096)
XLA Ops:
  7.9 53.2 %all-gather.6.cloned.1.call-done = bf16[2,2,64,8192]{3,2,1,0:T(8,128)(2,1)} async-done(((bf16[2,2,64,2048]{3,2,1,0:T(8,128)(2,1)}), bf16[2,2,64,8192]{3,2,1,0:T(8,128)(2,1)}) %all-gather.6.cloned.1.call-update) | async-done | bytes 4194320 | tf_op jit(solution)/shard_map/all_gather | solution.py:15
  61.1 4.0 copy.28
  65.2 4.4 copy.20
  69.6 6.7 %all-to-all-start = ((bf16[2,128,16,512]{3,1,0,2:T(8,128)(2,1)}), bf16[2,128,16,512]{3,1,0,2:T(8,128)(2,1)}, u32[]{:S(2)}, u32[]{:S(2)}) async-start(bf16[2,128,16,512]{3,1,0,2:T(8,128)(2,1)} %copy.20), calls=%async_computation | async-start | bytes 8388608 | tf_op jit(solution)/shard_map/all_to_all | solution.py:17
  76.4 1.2 collective-permute-start
  77.6 60.9 %all-to-all-done = bf16[2,128,16,512]{3,1,0,2:T(8,128)(2,1)} async-done(((bf16[2,128,16,512]{3,1,0,2:T(8,128)(2,1)}), bf16[2,128,16,512]{3,1,0,2:T(8,128)(2,1)}, u32[]{:S(2)}, u32[]{:S(2)}) %all-to-all-start) | async-done | bytes 4194336 | tf_op jit(solution)/shard_map/all_to_all | solution.py:17
  138.4 2.6 copy.21
  141.1 6.8 %convolution_convert_fusion = bf16[2048,2048]{1,0:T(8,128)(2,1)} fusion(bf16[2048,512]{1,0:T(8,128)(2,1)} %collective-permute-done, bf16[2,2048,512]{2,1,0:T(8,128)(2,1)S(1)} %bitcast.80, s32[]{:T(128)S(6)} %select_n.51, pred[]{:T(512)S(6)} %eq.3, bf16[1,2048,512]{2,1,0:T(8,128)(2,1)S(1)} %copy-done.3), kind=kOutput, calls=%fused_computation.2 | convolution fusion | flops 4300210176 | bytes 14680069 | tf_op jit(solution)/shard_map/dot_general | solution.py:45
  147.9 1.1 copy-done
  149.1 83.8 %reduce-scatter.2.cloned.1.call-done = bf16[128,2048]{1,0:T(8,128)(2,1)} async-done(((bf16[2048,2048]{1,0:T(8,128)(2,1)}), bf16[128,2048]{1,0:T(8,128)(2,1)}) %reduce-scatter.2.cloned.1.call-update) | async-done | bytes 524304 | tf_op jit(solution)/shard_map/reduce_scatter | solution.py:48
  232.9 2.0 fusion.8
  237.7 29.0 %all-gather.8.cloned.1.call-done = bf16[1,2,64,8192]{3,2,1,0:T(8,128)(2,1)} async-done(((bf16[1,2,64,2048]{3,2,1,0:T(8,128)(2,1)}), bf16[1,2,64,8192]{3,2,1,0:T(8,128)(2,1)}) %all-gather.8.cloned.1.call-update) | async-done | bytes 2097168 | tf_op jit(solution)/shard_map/all_gather | solution.py:15
  266.8 2.4 copy.29
  269.2 2.5 copy.24
  271.7 6.5 %all-to-all-start.1 = ((bf16[1,128,16,512]{3,1,0,2:T(8,128)(2,1)}), bf16[1,128,16,512]{3,1,0,2:T(8,128)(2,1)S(1)}, u32[]{:S(2)}, u32[]{:S(2)}) async-start(bf16[1,128,16,512]{3,1,0,2:T(8,128)(2,1)} %copy.24), calls=%async_computation.2 | async-start | bytes 4194304 | tf_op jit(solution)/shard_map/all_to_all | solution.py:17
  278.5 13.0 %psum.30 = f32[1,2,64,64]{3,2,1,0:T(8,128)S(1)} all-reduce(f32[1,2,64,64]{3,2,1,0:T(8,128)S(1)} %convolution_bitcast_fusion), channel_id=1, replica_groups=mesh['pipe'=2,'dp'=16,'tensor'=4] {'tensor'}, use_global_device_ids=true, to_apply=%region_3.4 | all-reduce | flops 8192 | bytes 65536 | tf_op jit(solution)/shard_map/psum | solution.py:22
  291.5 3.9 collective-permute-start.1
  296.1 13.4 %all-reduce.3.cloned.1.call-done = (f32[2,2,64,64]{3,2,1,0:T(8,128)}, f32[2,2,64,64]{3,2,1,0:T(8,128)}) async-done(((f32[2,2,64,64]{3,2,1,0:T(8,128)}, f32[2,2,64,64]{3,2,1,0:T(8,128)}), (f32[2,2,64,64]{3,2,1,0:T(8,128)}, f32[2,2,64,64]{3,2,1,0:T(8,128)})) %all-reduce.3.cloned.1.call-update) | async-done | bytes 131088 | tf_op jit(solution)/shard_map/psum | solution.py:22
  310.6 4.6 %psum.31 = f32[2,2]{1,0:T(2,128)S(1)} all-reduce(f32[2,2]{1,0:T(2,128)S(1)} %fusion.13), channel_id=1, replica_groups=mesh['pipe'=2,'dp'=16,'tensor'=4] {'pipe'}, use_global_device_ids=true, to_apply=%region_5.6 | all-reduce | flops 4 | bytes 32 | tf_op jit(solution)/shard_map/psum | solution.py:63
  315.7 19.6 %all-gather.1 = f32[16,2,2]{2,1,0:T(2,128)S(1)} all-gather(f32[1,2,2]{2,1,0:T(2,128)S(1)} %bitcast.84), channel_id=1, replica_groups=mesh['pipe'=2,'dp'=16,'tensor'=4] {'dp'}, dimensions={0}, use_global_device_ids=true | all-gather | bytes 272 | tf_op jit(solution)/shard_map/all_gather | solution.py:66
  335.9 88.8 %all-gather.10.cloned.1.call-done = bf16[1,2,32,64,2048]{4,3,2,1,0:T(8,128)(2,1)} async-done(((bf16[1,2,2,64,2048]{4,3,2,1,0:T(8,128)(2,1)}), bf16[1,2,32,64,2048]{4,3,2,1,0:T(8,128)(2,1)}) %all-gather.10.cloned.1.call-update) | async-done | bytes 16777232 | tf_op jit(solution)/shard_map/all_gather | solution.py:38
  424.8 9.8 %fusion = bf16[2,32,64,2048]{3,2,1,0:T(8,128)(2,1)S(1)} fusion(bf16[1,2,32,64,2048]{4,3,2,1,0:T(8,128)(2,1)} %all-gather.10.cloned.1.call-done, f32[2,32]{1,0:T(2,128)S(1)} %bitcast.83), kind=kLoop, calls=%fused_computation.1 | loop fusion | flops 25165824 | bytes 33554688 | tf_op jit(solution)/shard_map/convert_element_type | solution.py:75
  434.6 3.9 fusion.1
  438.5 11.6 %fusion.3 = f32[1,2048,512]{2,1,0:T(8,128)} fusion(bf16[1,2048,512]{2,1,0:T(8,128)(2,1)} %param.9, bf16[4096,2048]{1,0:T(8,128)(2,1)S(1)} %bitcast.71, bf16[4096,512]{1,0:T(8,128)(2,1)S(1)} %bitcast.79, f32[]{:T(128)S(6)} %mul_shard_map.3), kind=kOutput, calls=%fused_computation.7 | convolution fusion | flops 8594128896 | bytes 27262980 | tf_op jit(solution)/shard_map/dot_general | solution.py:80
  (31 shorter events, 6.1 us)
Async XLA Ops:
  7.2 54.0 %all-gather.6.cloned.1.call-start = ((), (), s32[]{:S(2)}) async-start(), calls=%async_computation.3 | async-start | bytes 5242880 | tf_op jit(solution)/shard_map/all_gather | solution.py:15
  69.6 6.8 %copy-start.3 = (bf16[1,2048,512]{2,1,0:T(8,128)(2,1)S(1)}, bf16[1,2048,512]{2,1,0:T(8,128)(2,1)}, u32[]{:S(2)}) copy-start(bf16[1,2048,512]{2,1,0:T(8,128)(2,1)} %param.5) | copy-start | bytes 6291460
  69.6 68.8 %all-to-all-start = ((bf16[2,128,16,512]{3,1,0,2:T(8,128)(2,1)}), bf16[2,128,16,512]{3,1,0,2:T(8,128)(2,1)}, u32[]{:S(2)}, u32[]{:S(2)}) async-start(bf16[2,128,16,512]{3,1,0,2:T(8,128)(2,1)} %copy.20), calls=%async_computation | async-start | bytes 8388608 | tf_op jit(solution)/shard_map/all_to_all | solution.py:17
  76.3 156.6 %reduce-scatter.2.cloned.1.call-start = ((), (), s32[]{:S(2)}) async-start(), calls=%async_computation.4 | async-start | bytes 8912896 | tf_op jit(solution)/shard_map/reduce_scatter | solution.py:48
  76.4 64.7 %collective-permute-start = (bf16[2048,512]{1,0:T(8,128)(2,1)S(1)}, bf16[2048,512]{1,0:T(8,128)(2,1)}, u32[]{:S(2)}, u32[]{:S(2)}) collective-permute-start(bf16[2048,512]{1,0:T(8,128)(2,1)S(1)} %bitcast.85), channel_id=1, source_target_pairs={{0,64},{64,0},{1,65},{65,1},{2,66},{66,2},{3,67},{67,3},{4,68},{68... | collective-permute-start | bytes 6291464 | tf_op jit(solution)/shard_map/ppermute | solution.py:9
  147.9 1.2 copy-start
  147.9 87.1 %copy-start.2 = (bf16[1,2,2,64,2048]{4,3,2,1,0:T(8,128)(2,1)S(1)}, bf16[1,2,2,64,2048]{4,3,2,1,0:T(8,128)(2,1)}, u32[]{:S(2)}) copy-start(bf16[1,2,2,64,2048]{4,3,2,1,0:T(8,128)(2,1)} %param.6) | copy-start | bytes 3145732
  147.9 118.9 %all-gather.8.cloned.1.call-start = ((), (), s32[]{:S(2)}) async-start(), calls=%async_computation.5 | async-start | bytes 2621440 | tf_op jit(solution)/shard_map/all_gather | solution.py:15
  234.9 74.6 %all-reduce.3.cloned.1.call-start = ((), (), s32[]{:S(2)}) async-start(), calls=%async_computation.7 | async-start | bytes 524288 | tf_op jit(solution)/shard_map/psum | solution.py:22
  237.1 187.6 %all-gather.10.cloned.1.call-start = ((), (), s32[]{:S(2)}) async-start(), calls=%async_computation.6 | async-start | bytes 17825792 | tf_op jit(solution)/shard_map/all_gather | solution.py:38
  269.2 9.0 %copy-start.1 = (bf16[128,2048]{1,0:T(8,128)(2,1)S(1)}, bf16[128,2048]{1,0:T(8,128)(2,1)}, u32[]{:S(2)}) copy-start(bf16[128,2048]{1,0:T(8,128)(2,1)} %fusion.8) | copy-start | bytes 1572868
  271.7 43.6 %all-to-all-start.1 = ((bf16[1,128,16,512]{3,1,0,2:T(8,128)(2,1)}), bf16[1,128,16,512]{3,1,0,2:T(8,128)(2,1)S(1)}, u32[]{:S(2)}, u32[]{:S(2)}) async-start(bf16[1,128,16,512]{3,1,0,2:T(8,128)(2,1)} %copy.24), calls=%async_computation.2 | async-start | bytes 4194304 | tf_op jit(solution)/shard_map/all_to_all | solution.py:17
  291.5 18.0 %collective-permute-start.1 = (f32[1,2,64,64]{3,2,1,0:T(8,128)S(1)}, f32[1,2,64,64]{3,2,1,0:T(8,128)S(1)}, u32[]{:S(2)}, u32[]{:S(2)}) collective-permute-start(f32[1,2,64,64]{3,2,1,0:T(8,128)S(1)} %psum.30), channel_id=1, source_target_pairs={{0,64},{64,0},{1,65},{65,1},{2,66},{66,2},{3,67},{67,3},{4,68},{68... | collective-permute-start | bytes 98312 | tf_op jit(solution)/shard_map/ppermute | solution.py:9
  315.3 119.3 %collective-permute-start.2 = (bf16[1,2048,512]{2,1,0:T(8,128)(2,1)S(1)}, bf16[1,2048,512]{2,1,0:T(8,128)(2,1)}, u32[]{:S(2)}, u32[]{:S(2)}) collective-permute-start(bf16[1,2048,512]{2,1,0:T(8,128)(2,1)S(1)} %bitcast.73), channel_id=1, source_target_pairs={{0,64},{64,0},{1,65},{65,1},{2,66},{66,2},{3,67},{67,3},{4,68},{68... | collective-permute-start | bytes 6291464 | tf_op jit(solution)/shard_map/ppermute | solution.py:9
Sparse Core Ops, SparseCore 0:
  9.6 51.4 all-gather.5
  148.0 84.8 reduce-scatter.1
  235.0 31.6 all-gather.7
  269.0 40.4 all-reduce.2
  311.5 113.2 all-gather.9
where the time goes:
time: 457 us
  waiting for transfers between devices  330 us (72%)
  blocking collectives  37.2 us (8%)
  matrix products  20.8 us (5%)
  starting transfers between devices  18.9 us (4%)
  local copies, waits for them, and re-layouts  17.4 us (4%)
  other arithmetic  17.4 us (4%)
  between operations  14.6 us (3%)
    all_gather x1, waiting for transfers between devices, local(): gathered_inputs = lax.all_gather(local_inputs, 'dp', axis=1, tiled=True)  88.8 us
    reduce_scatter x1, waiting for transfers between devices, local(): lax.psum_scatter(terms, 'dp', scatter_dimension=0, tiled=True)  83.8 us
    all_gather x2, waiting for transfers between devices, to_column_blocks(): full = lax.all_gather(values, 'tensor', axis=3, tiled=True)  82.3 us
    all_to_all x2, waiting for transfers between devices, to_column_blocks(): lax.all_to_all(by_block, 'dp', split_axis=2, concat_axis=1, tiled=True)  60.9 us
    all_gather x1, blocking collectives, local(): all_scales = lax.all_gather(scale_terms, 'dp', axis=1, tiled=True)  19.6 us
    psum x1, waiting for transfers between devices, grams(): lax.psum(jnp.einsum('...ld,...kd->...lk', values, values, preferred_eleme...  13.4 us
    all_to_all x2, starting transfers between devices, to_column_blocks(): lax.all_to_all(by_block, 'dp', split_axis=2, concat_axis=1, tiled=True)  13.2 us
    psum x1, blocking collectives, grams(): lax.psum(jnp.einsum('...ld,...kd->...lk', values, values, preferred_eleme...  13 us
  transfers between devices with their start and end apart: 10, of which 6 were waited for; matrix products, arithmetic and copies ran while one was open for 5% of the time, Pallas kernels for 0%

commit v1 on v0

--- a/solution.py
+++ b/solution.py
@@ -2,6 +2,27 @@
 import jax.numpy as jnp
 from jax import lax
 from jax.sharding import PartitionSpec as P
+
+
+def replace_the_unit(point, mesh_ax, dim_k=1):
+    out_arr, z2, y2 = (lax.axis_size(mesh_ax), lax.axis_index(mesh_ax), point.shape[dim_k])
+    pile = [(ii, (ii + 1) % out_arr) for ii in range(out_arr)]
+    trail = [(ii, (ii - 1) % out_arr) for ii in range(out_arr)]
+    oldest = jnp.zeros((*point.shape[:dim_k], out_arr * y2, *point.shape[dim_k + 1 :]), point.dtype)
+    x_next = b_next = point
+    oldest = lax.dynamic_update_slice_in_dim(oldest, point, z2 * y2, axis=dim_k)
+    local_out = out_arr // 2
+    for no in range(1, local_out + 1):
+        x_next = lax.ppermute(x_next, mesh_ax, pile)
+        oldest = lax.dynamic_update_slice_in_dim(
+            oldest, x_next, (z2 - no) % out_arr * y2, axis=dim_k
+        )
+        if no < out_arr - local_out:
+            b_next = lax.ppermute(b_next, mesh_ax, trail)
+            oldest = lax.dynamic_update_slice_in_dim(
+                oldest, b_next, (z2 + no) % out_arr * y2, axis=dim_k
+            )
+    return oldest
 
 
 def swapped(value, axis):
@@ -35,7 +56,7 @@
     column_part = weight_block.shape[1]
     full_width = column_part * group_count
     is_last = section_index == 1
-    gathered_inputs = lax.all_gather(local_inputs, "dp", axis=1, tiled=True)
+    gathered_inputs = replace_the_unit(local_inputs, "dp")
     input_grams = grams(local_inputs)
     last_grams = grams(cotangent)
     last_blocks = to_column_blocks(cotangent, group_count, column_part)

time: 457 us -> 502 us (1.098); the launches traced: 457 us -> 496 us
  waiting for transfers between devices: 330 us -> 277 us
  starting transfers between devices: 18.9 us -> 71.3 us
  local copies, waits for them, and re-layouts: 17.4 us -> 57.7 us
    ppermute x0 -> x15, waiting for transfers between devices: none -> 95.7 us  [the longest x7 57.4 us: replace_the_unit(): b_next = lax.ppermute(b_next, mesh_ax, trail)]
    all_gather x1 -> x0, waiting for transfers between devices: 88.8 us -> none  [local(): gathered_inputs = lax.all_gather(local_inputs, 'dp', axis=1, tiled=True)]
    dynamic_update_slice x0 -> x16, local copies, waits for them, and re-layouts: none -> 34.5 us  [the longest x8 17.2 us: replace_the_unit(): lax.dynamic_update_slice_in_dim(oldest, x_next, (z2 - no) % out_arr * y2,...]
    ppermute x0 -> x15, starting transfers between devices: none -> 34.1 us  [the longest x7 34 us: replace_the_unit(): b_next = lax.ppermute(b_next, mesh_ax, trail)]
    all_gather x2, waiting for transfers between devices: 82.3 us -> 53.2 us  [to_column_blocks(): full = lax.all_gather(values, 'tensor', axis=3, tiled=True)]
    ppermute x3, starting transfers between devices: 5.45 us -> 24.3 us  [swapped(): lax.ppermute(value, axis, [(source, count - 1 - source) for source in ran...]
    reduce_scatter x1, waiting for transfers between devices: 83.8 us -> 66.2 us  [local(): lax.psum_scatter(terms, 'dp', scatter_dimension=0, tiled=True)]
    psum x1, waiting for transfers between devices: 13.4 us -> 0.01 us  [grams(): lax.psum(jnp.einsum('...ld,...kd->...lk', values, values, preferred_eleme...]
  transfers between devices with their start and end apart: 10 -> 24, of which waited for: 6 -> 10; matrix products, arithmetic and copies ran while one was open for 5% -> 13% of each run, Pallas kernels for 0% -> 0%
where the time goes in v1:
time: 502 us; the launch traced here: 496 us
  waiting for transfers between devices  277 us (55%)
  starting transfers between devices  71.3 us (14%)
  local copies, waits for them, and re-layouts  57.7 us (11%)
  blocking collectives  35.6 us (7%)
  matrix products  22.6 us (5%)
  other arithmetic  17.4 us (3%)
  between operations  14.6 us (3%)
    reduce_scatter x1, waiting for transfers between devices, local(): lax.psum_scatter(terms, 'dp', scatter_dimension=0, tiled=True)  66.2 us
    all_to_all x2, waiting for transfers between devices, to_column_blocks(): lax.all_to_all(by_block, 'dp', split_axis=2, concat_axis=1, tiled=True)  60.9 us
    ppermute x7, waiting for transfers between devices, replace_the_unit(): b_next = lax.ppermute(b_next, mesh_ax, trail)  57.4 us
    all_gather x2, waiting for transfers between devices, to_column_blocks(): full = lax.all_gather(values, 'tensor', axis=3, tiled=True)  53.2 us
    ppermute x8, waiting for transfers between devices, replace_the_unit(): x_next = lax.ppermute(x_next, mesh_ax, pile)  38.3 us
    ppermute x7, starting transfers between devices, replace_the_unit(): b_next = lax.ppermute(b_next, mesh_ax, trail)  34 us
    ppermute x3, starting transfers between devices, swapped(): lax.ppermute(value, axis, [(source, count - 1 - source) for source in ran...  24.3 us
    dynamic_update_slice x8, local copies, waits for them, and re-layouts, replace_the_unit(): lax.dynamic_update_slice_in_dim(oldest, x_next, (z2 - no) % out_arr * y2,...  17.2 us
  transfers between devices with their start and end apart: 24, of which 10 were waited for; matrix products, arithmetic and copies ran while one was open for 13% of the time, Pallas kernels for 0%

profile of v1, /device:TPU:1, one launch (start us, length us, event | category | flops | bytes accessed | tf_op | source)
XLA Modules:
  0.0 495.9 jit_solution(10785329222205550542)
XLA Ops:
  7.9 53.2 %all-gather.4.cloned.1.call-done = bf16[2,2,64,8192]{3,2,1,0:T(8,128)(2,1)} async-done(((bf16[2,2,64,2048]{3,2,1,0:T(8,128)(2,1)}), bf16[2,2,64,8192]{3,2,1,0:T(8,128)(2,1)}) %all-gather.4.cloned.1.call-update) | async-done | bytes 4194320 | tf_op jit(solution)/shard_map/all_gather | solution.py:36
  69.6 6.6 %all-to-all-start = ((bf16[2,128,16,512]{3,1,0,2:T(8,128)(2,1)}), bf16[2,128,16,512]{3,1,0,2:T(8,128)(2,1)}, u32[]{:S(2)}, u32[]{:S(2)}) async-start(bf16[2,128,16,512]{3,1,0,2:T(8,128)(2,1)} %copy.20), calls=%async_computation | async-start | bytes 8388608 | tf_op jit(solution)/shard_map/all_to_all | solution.py:38
  77.4 60.9 %all-to-all-done = bf16[2,128,16,512]{3,1,0,2:T(8,128)(2,1)} async-done(((bf16[2,128,16,512]{3,1,0,2:T(8,128)(2,1)}), bf16[2,128,16,512]{3,1,0,2:T(8,128)(2,1)}, u32[]{:S(2)}, u32[]{:S(2)}) %all-to-all-start) | async-done | bytes 4194336 | tf_op jit(solution)/shard_map/all_to_all | solution.py:38
  141.0 8.6 %convolution_convert_fusion = bf16[2048,2048]{1,0:T(8,128)(2,1)} fusion(bf16[2048,512]{1,0:T(8,128)(2,1)} %collective-permute-done.15, bf16[2,2048,512]{2,1,0:T(8,128)(2,1)S(1)} %bitcast.78, s32[]{:T(128)S(6)} %select_n.193, pred[]{:T(512)S(6)} %eq.19, bf16[1,2048,512]{2,1,0:T(8,128)(2,1)} %param.5), kind=kOutput, calls=%fused_computation.1 | convolution fusion | flops 4300210176 | bytes 14680069 | tf_op jit(solution)/shard_map/dot_general | solution.py:66
  149.7 4.8 collective-permute-start.1
  154.5 31.4 %collective-permute-done = bf16[2,2,64,2048]{3,2,1,0:T(8,128)(2,1)} collective-permute-done((bf16[2,2,64,2048]{3,2,1,0:T(8,128)(2,1)S(1)}, bf16[2,2,64,2048]{3,2,1,0:T(8,128)(2,1)}, u32[]{:S(2)}, u32[]{:S(2)}) %collective-permute-start) | collective-permute-done | bytes 1048608 | tf_op jit(solution)/shard_map/ppermute | solution.py:16
  185.9 66.2 %reduce-scatter.2.cloned.1.call-done = bf16[128,2048]{1,0:T(8,128)(2,1)} async-done(((bf16[2048,2048]{1,0:T(8,128)(2,1)}), bf16[128,2048]{1,0:T(8,128)(2,1)}) %reduce-scatter.2.cloned.1.call-update) | async-done | bytes 524304 | tf_op jit(solution)/shard_map/reduce_scatter | solution.py:69
  256.6 20.8 %collective-permute-done.3 = bf16[2,2,64,2048]{3,2,1,0:T(8,128)(2,1)} collective-permute-done((bf16[2,2,64,2048]{3,2,1,0:T(8,128)(2,1)}, bf16[2,2,64,2048]{3,2,1,0:T(8,128)(2,1)}, u32[]{:S(2)}, u32[]{:S(2)}) %collective-permute-start.3) | collective-permute-done | bytes 1048608 | tf_op jit(solution)/shard_map/ppermute | solution.py:21
  277.4 5.5 %collective-permute-start.5 = (bf16[2,2,64,2048]{3,2,1,0:T(8,128)(2,1)}, bf16[2,2,64,2048]{3,2,1,0:T(8,128)(2,1)}, u32[]{:S(2)}, u32[]{:S(2)}) collective-permute-start(bf16[2,2,64,2048]{3,2,1,0:T(8,128)(2,1)} %collective-permute-done.3), channel_id=1, source_target_pairs={{0,60},{4,0},{8,4},{12,8},{16,12},{20,16},{24,20},{28,24},{32,28},... | collective-permute-start | bytes 3145736 | tf_op jit(solution)/shard_map/ppermute | solution.py:21
  283.9 19.0 %collective-permute-done.5 = bf16[2,2,64,2048]{3,2,1,0:T(8,128)(2,1)} collective-permute-done((bf16[2,2,64,2048]{3,2,1,0:T(8,128)(2,1)}, bf16[2,2,64,2048]{3,2,1,0:T(8,128)(2,1)}, u32[]{:S(2)}, u32[]{:S(2)}) %collective-permute-start.5) | collective-permute-done | bytes 1048608 | tf_op jit(solution)/shard_map/ppermute | solution.py:21
  302.8 5.5 %collective-permute-start.7 = (bf16[2,2,64,2048]{3,2,1,0:T(8,128)(2,1)}, bf16[2,2,64,2048]{3,2,1,0:T(8,128)(2,1)}, u32[]{:S(2)}, u32[]{:S(2)}) collective-permute-start(bf16[2,2,64,2048]{3,2,1,0:T(8,128)(2,1)} %collective-permute-done.5), channel_id=1, source_target_pairs={{0,60},{4,0},{8,4},{12,8},{16,12},{20,16},{24,20},{28,24},{32,28},... | collective-permute-start | bytes 3145736 | tf_op jit(solution)/shard_map/ppermute | solution.py:21
  311.0 16.4 %collective-permute-done.7 = bf16[2,2,64,2048]{3,2,1,0:T(8,128)(2,1)} collective-permute-done((bf16[2,2,64,2048]{3,2,1,0:T(8,128)(2,1)}, bf16[2,2,64,2048]{3,2,1,0:T(8,128)(2,1)}, u32[]{:S(2)}, u32[]{:S(2)}) %collective-permute-start.7) | collective-permute-done | bytes 1048608 | tf_op jit(solution)/shard_map/ppermute | solution.py:21
  327.5 5.5 %collective-permute-start.9 = (bf16[2,2,64,2048]{3,2,1,0:T(8,128)(2,1)}, bf16[2,2,64,2048]{3,2,1,0:T(8,128)(2,1)}, u32[]{:S(2)}, u32[]{:S(2)}) collective-permute-start(bf16[2,2,64,2048]{3,2,1,0:T(8,128)(2,1)} %collective-permute-done.7), channel_id=1, source_target_pairs={{0,60},{4,0},{8,4},{12,8},{16,12},{20,16},{24,20},{28,24},{32,28},... | collective-permute-start | bytes 3145736 | tf_op jit(solution)/shard_map/ppermute | solution.py:21
  333.0 6.0 %broadcast_in_dim.7 = bf16[2,32,64,2048]{3,2,1,0:T(8,128)(2,1)} broadcast(bf16[]{:T(256)} %constant.105.clone.1), dimensions={} | broadcast | bytes 16777218 | tf_op jit(solution)/shard_map/broadcast_in_dim | solution.py:11
  351.2 5.5 %collective-permute-start.11 = (bf16[2,2,64,2048]{3,2,1,0:T(8,128)(2,1)}, bf16[2,2,64,2048]{3,2,1,0:T(8,128)(2,1)}, u32[]{:S(2)}, u32[]{:S(2)}) collective-permute-start(bf16[2,2,64,2048]{3,2,1,0:T(8,128)(2,1)} %collective-permute-done.9), channel_id=1, source_target_pairs={{0,60},{4,0},{8,4},{12,8},{16,12},{20,16},{24,20},{28,24},{32,28},... | collective-permute-start | bytes 3145736 | tf_op jit(solution)/shard_map/ppermute | solution.py:21
  360.1 6.4 %collective-permute-done.10 = bf16[2,2,64,2048]{3,2,1,0:T(8,128)(2,1)} collective-permute-done((bf16[2,2,64,2048]{3,2,1,0:T(8,128)(2,1)}, bf16[2,2,64,2048]{3,2,1,0:T(8,128)(2,1)}, u32[]{:S(2)}, u32[]{:S(2)}) %collective-permute-start.10) | collective-permute-done | bytes 1048608 | tf_op jit(solution)/shard_map/ppermute | solution.py:16
  376.0 6.2 %all-to-all-start.1 = ((bf16[1,128,16,512]{3,1,0,2:T(8,128)(2,1)}), bf16[1,128,16,512]{3,1,0,2:T(8,128)(2,1)S(1)}, u32[]{:S(2)}, u32[]{:S(2)}) async-start(bf16[1,128,16,512]{3,1,0,2:T(8,128)(2,1)} %copy.24), calls=%async_computation.2 | async-start | bytes 4194304 | tf_op jit(solution)/shard_map/all_to_all | solution.py:38
  384.6 4.7 collective-permute-start.13
  398.8 14.9 %psum.30 = f32[1,2,64,64]{3,2,1,0:T(8,128)S(1)} all-reduce(f32[1,2,64,64]{3,2,1,0:T(8,128)S(1)} %convolution_bitcast_fusion), channel_id=1, replica_groups=mesh['pipe'=2,'dp'=16,'tensor'=4] {'tensor'}, use_global_device_ids=true, to_apply=%region_3.4 | all-reduce | flops 8192 | bytes 65536 | tf_op jit(solution)/shard_map/psum | solution.py:43
  413.7 22.7 %collective-permute-start.16 = (f32[1,2,64,64]{3,2,1,0:T(8,128)S(1)}, f32[1,2,64,64]{3,2,1,0:T(8,128)S(1)}, u32[]{:S(2)}, u32[]{:S(2)}) collective-permute-start(f32[1,2,64,64]{3,2,1,0:T(8,128)S(1)} %psum.30), channel_id=1, source_target_pairs={{0,64},{64,0},{1,65},{65,1},{2,66},{66,2},{3,67},{67,3},{4,68},{68... | collective-permute-start | bytes 98312 | tf_op jit(solution)/shard_map/ppermute | solution.py:30
  442.2 5.9 %psum.31 = f32[2,2]{1,0:T(2,128)S(1)} all-reduce(f32[2,2]{1,0:T(2,128)S(1)} %fusion.10), channel_id=1, replica_groups=mesh['pipe'=2,'dp'=16,'tensor'=4] {'pipe'}, use_global_device_ids=true, to_apply=%region_5.6 | all-reduce | flops 4 | bytes 32 | tf_op jit(solution)/shard_map/psum | solution.py:84
  448.5 14.9 %all-gather = f32[16,2,2]{2,1,0:T(2,128)S(1)} all-gather(f32[1,2,2]{2,1,0:T(2,128)S(1)} %bitcast.84), channel_id=1, replica_groups=mesh['pipe'=2,'dp'=16,'tensor'=4] {'dp'}, dimensions={0}, use_global_device_ids=true | all-gather | bytes 272 | tf_op jit(solution)/shard_map/all_gather | solution.py:87
  464.0 9.8 %multiply_convert_fusion = bf16[2,32,64,2048]{3,2,1,0:T(8,128)(2,1)S(1)} fusion(bf16[2,32,64,2048]{3,2,1,0:T(8,128)(2,1)} %constant_dynamic-update-slice_fusion, f32[2,32]{1,0:T(2,128)S(1)} %bitcast.83), kind=kLoop, calls=%fused_computation | loop fusion | flops 25165824 | bytes 33554688 | tf_op jit(solution)/shard_map/convert_element_type | solution.py:96
  477.8 11.6 %fusion.2 = f32[1,2048,512]{2,1,0:T(8,128)} fusion(bf16[1,2048,512]{2,1,0:T(8,128)(2,1)} %param.9, bf16[4096,2048]{1,0:T(8,128)(2,1)S(1)} %bitcast.69, bf16[4096,512]{1,0:T(8,128)(2,1)S(1)} %bitcast.77, f32[]{:T(128)S(6)} %mul_shard_map.3), kind=kOutput, calls=%fused_computation.6 | convolution fusion | flops 8594128896 | bytes 27262980 | tf_op jit(solution)/shard_map/dot_general | solution.py:101
  (79 shorter events, 68.4 us)
Async XLA Ops:
  7.2 54.0 %all-gather.4.cloned.1.call-start = ((), (), s32[]{:S(2)}) async-start(), calls=%async_computation.3 | async-start | bytes 5242880 | tf_op jit(solution)/shard_map/all_gather | solution.py:36
  69.6 68.7 %all-to-all-start = ((bf16[2,128,16,512]{3,1,0,2:T(8,128)(2,1)}), bf16[2,128,16,512]{3,1,0,2:T(8,128)(2,1)}, u32[]{:S(2)}, u32[]{:S(2)}) async-start(bf16[2,128,16,512]{3,1,0,2:T(8,128)(2,1)} %copy.20), calls=%async_computation | async-start | bytes 8388608 | tf_op jit(solution)/shard_map/all_to_all | solution.py:38
  76.2 175.9 %reduce-scatter.2.cloned.1.call-start = ((), (), s32[]{:S(2)}) async-start(), calls=%async_computation.4 | async-start | bytes 8912896 | tf_op jit(solution)/shard_map/reduce_scatter | solution.py:69
  76.2 64.7 %collective-permute-start.15 = (bf16[2048,512]{1,0:T(8,128)(2,1)S(1)}, bf16[2048,512]{1,0:T(8,128)(2,1)}, u32[]{:S(2)}, u32[]{:S(2)}) collective-permute-start(bf16[2048,512]{1,0:T(8,128)(2,1)S(1)} %bitcast.85), channel_id=1, source_target_pairs={{0,64},{64,0},{1,65},{65,1},{2,66},{66,2},{3,67},{67,3},{4,68},{68... | collective-permute-start | bytes 6291464 | tf_op jit(solution)/shard_map/ppermute | solution.py:30
  149.6 221.6 %all-gather.6.cloned.1.call-start = ((), (), s32[]{:S(2)}) async-start(), calls=%async_computation.5 | async-start | bytes 2621440 | tf_op jit(solution)/shard_map/all_gather | solution.py:36
  149.6 36.2 %collective-permute-start = (bf16[2,2,64,2048]{3,2,1,0:T(8,128)(2,1)S(1)}, bf16[2,2,64,2048]{3,2,1,0:T(8,128)(2,1)}, u32[]{:S(2)}, u32[]{:S(2)}) collective-permute-start(bf16[2,2,64,2048]{3,2,1,0:T(8,128)(2,1)S(1)} %bitcast.80), channel_id=1, source_target_pairs={{0,4},{4,8},{8,12},{12,16},{16,20},{20,24},{24,28},{28,32},{32,36}... | collective-permute-start | bytes 3145736 | tf_op jit(solution)/shard_map/ppermute | solution.py:16
  149.7 104.4 %collective-permute-start.1 = (bf16[2,2,64,2048]{3,2,1,0:T(8,128)(2,1)S(1)}, bf16[2,2,64,2048]{3,2,1,0:T(8,128)(2,1)}, u32[]{:S(2)}, u32[]{:S(2)}) collective-permute-start(bf16[2,2,64,2048]{3,2,1,0:T(8,128)(2,1)S(1)} %bitcast.81), channel_id=1, source_target_pairs={{0,60},{4,0},{8,4},{12,8},{16,12},{20,16},{24,20},{28,24},{32,28},... | collective-permute-start | bytes 3145736 | tf_op jit(solution)/shard_map/ppermute | solution.py:21
  185.8 70.8 %collective-permute-start.2 = (bf16[2,2,64,2048]{3,2,1,0:T(8,128)(2,1)}, bf16[2,2,64,2048]{3,2,1,0:T(8,128)(2,1)}, u32[]{:S(2)}, u32[]{:S(2)}) collective-permute-start(bf16[2,2,64,2048]{3,2,1,0:T(8,128)(2,1)} %collective-permute-done), channel_id=1, source_target_pairs={{0,4},{4,8},{8,12},{12,16},{16,20},{20,24},{24,28},{28,32},{32,36}... | collective-permute-start | bytes 3145736 | tf_op jit(solution)/shard_map/ppermute | solution.py:16
  254.0 184.7 %all-reduce.3.cloned.1.call-start = ((), (), s32[]{:S(2)}) async-start(), calls=%async_computation.6 | async-start | bytes 524288 | tf_op jit(solution)/shard_map/psum | solution.py:43
  254.1 23.3 %collective-permute-start.3 = (bf16[2,2,64,2048]{3,2,1,0:T(8,128)(2,1)}, bf16[2,2,64,2048]{3,2,1,0:T(8,128)(2,1)}, u32[]{:S(2)}, u32[]{:S(2)}) collective-permute-start(bf16[2,2,64,2048]{3,2,1,0:T(8,128)(2,1)} %collective-permute-done.1), channel_id=1, source_target_pairs={{0,60},{4,0},{8,4},{12,8},{16,12},{20,16},{24,20},{28,24},{32,28},... | collective-permute-start | bytes 3145736 | tf_op jit(solution)/shard_map/ppermute | solution.py:21
  256.6 26.3 %collective-permute-start.4 = (bf16[2,2,64,2048]{3,2,1,0:T(8,128)(2,1)}, bf16[2,2,64,2048]{3,2,1,0:T(8,128)(2,1)S(1)}, u32[]{:S(2)}, u32[]{:S(2)}) collective-permute-start(bf16[2,2,64,2048]{3,2,1,0:T(8,128)(2,1)} %collective-permute-done.2), channel_id=1, source_target_pairs={{0,4},{4,8},{8,12},{12,16},{16,20},{20,24},{24,28},{28,32},{32,36}... | collective-permute-start | bytes 3145736 | tf_op jit(solution)/shard_map/ppermute | solution.py:16
  277.4 25.5 %collective-permute-start.5 = (bf16[2,2,64,2048]{3,2,1,0:T(8,128)(2,1)}, bf16[2,2,64,2048]{3,2,1,0:T(8,128)(2,1)}, u32[]{:S(2)}, u32[]{:S(2)}) collective-permute-start(bf16[2,2,64,2048]{3,2,1,0:T(8,128)(2,1)} %collective-permute-done.3), channel_id=1, source_target_pairs={{0,60},{4,0},{8,4},{12,8},{16,12},{20,16},{24,20},{28,24},{32,28},... | collective-permute-start | bytes 3145736 | tf_op jit(solution)/shard_map/ppermute | solution.py:21
  283.9 25.0 %collective-permute-start.6 = (bf16[2,2,64,2048]{3,2,1,0:T(8,128)(2,1)S(1)}, bf16[2,2,64,2048]{3,2,1,0:T(8,128)(2,1)}, u32[]{:S(2)}, u32[]{:S(2)}) collective-permute-start(bf16[2,2,64,2048]{3,2,1,0:T(8,128)(2,1)S(1)} %collective-permute-done.4), channel_id=1, source_target_pairs={{0,4},{4,8},{8,12},{12,16},{16,20},{20,24},{24,28},{28,32},{32,36}... | collective-permute-start | bytes 3145736 | tf_op jit(solution)/shard_map/ppermute | solution.py:16
  302.8 24.6 %collective-permute-start.7 = (bf16[2,2,64,2048]{3,2,1,0:T(8,128)(2,1)}, bf16[2,2,64,2048]{3,2,1,0:T(8,128)(2,1)}, u32[]{:S(2)}, u32[]{:S(2)}) collective-permute-start(bf16[2,2,64,2048]{3,2,1,0:T(8,128)(2,1)} %collective-permute-done.5), channel_id=1, source_target_pairs={{0,60},{4,0},{8,4},{12,8},{16,12},{20,16},{24,20},{28,24},{32,28},... | collective-permute-start | bytes 3145736 | tf_op jit(solution)/shard_map/ppermute | solution.py:21
  308.8 34.2 %collective-permute-start.8 = (bf16[2,2,64,2048]{3,2,1,0:T(8,128)(2,1)}, bf16[2,2,64,2048]{3,2,1,0:T(8,128)(2,1)}, u32[]{:S(2)}, u32[]{:S(2)}) collective-permute-start(bf16[2,2,64,2048]{3,2,1,0:T(8,128)(2,1)} %collective-permute-done.6), channel_id=1, source_target_pairs={{0,4},{4,8},{8,12},{12,16},{16,20},{20,24},{24,28},{28,32},{32,36}... | collective-permute-start | bytes 3145736 | tf_op jit(solution)/shard_map/ppermute | solution.py:16
  327.5 23.8 %collective-permute-start.9 = (bf16[2,2,64,2048]{3,2,1,0:T(8,128)(2,1)}, bf16[2,2,64,2048]{3,2,1,0:T(8,128)(2,1)}, u32[]{:S(2)}, u32[]{:S(2)}) collective-permute-start(bf16[2,2,64,2048]{3,2,1,0:T(8,128)(2,1)} %collective-permute-done.7), channel_id=1, source_target_pairs={{0,60},{4,0},{8,4},{12,8},{16,12},{20,16},{24,20},{28,24},{32,28},... | collective-permute-start | bytes 3145736 | tf_op jit(solution)/shard_map/ppermute | solution.py:21
  343.0 23.5 %collective-permute-start.10 = (bf16[2,2,64,2048]{3,2,1,0:T(8,128)(2,1)}, bf16[2,2,64,2048]{3,2,1,0:T(8,128)(2,1)}, u32[]{:S(2)}, u32[]{:S(2)}) collective-permute-start(bf16[2,2,64,2048]{3,2,1,0:T(8,128)(2,1)} %collective-permute-done.8), channel_id=1, source_target_pairs={{0,4},{4,8},{8,12},{12,16},{16,20},{20,24},{24,28},{28,32},{32,36}... | collective-permute-start | bytes 3145736 | tf_op jit(solution)/shard_map/ppermute | solution.py:16
  351.2 33.4 %collective-permute-start.11 = (bf16[2,2,64,2048]{3,2,1,0:T(8,128)(2,1)}, bf16[2,2,64,2048]{3,2,1,0:T(8,128)(2,1)}, u32[]{:S(2)}, u32[]{:S(2)}) collective-permute-start(bf16[2,2,64,2048]{3,2,1,0:T(8,128)(2,1)} %collective-permute-done.9), channel_id=1, source_target_pairs={{0,60},{4,0},{8,4},{12,8},{16,12},{20,16},{24,20},{28,24},{32,28},... | collective-permute-start | bytes 3145736 | tf_op jit(solution)/shard_map/ppermute | solution.py:21
  366.5 27.4 %collective-permute-start.12 = (bf16[2,2,64,2048]{3,2,1,0:T(8,128)(2,1)}, bf16[2,2,64,2048]{3,2,1,0:T(8,128)(2,1)}, u32[]{:S(2)}, u32[]{:S(2)}) collective-permute-start(bf16[2,2,64,2048]{3,2,1,0:T(8,128)(2,1)} %collective-permute-done.10), channel_id=1, source_target_pairs={{0,4},{4,8},{8,12},{12,16},{16,20},{20,24},{24,28},{28,32},{32,36}... | collective-permute-start | bytes 3145736 | tf_op jit(solution)/shard_map/ppermute | solution.py:16
  376.0 72.0 %all-to-all-start.1 = ((bf16[1,128,16,512]{3,1,0,2:T(8,128)(2,1)}), bf16[1,128,16,512]{3,1,0,2:T(8,128)(2,1)S(1)}, u32[]{:S(2)}, u32[]{:S(2)}) async-start(bf16[1,128,16,512]{3,1,0,2:T(8,128)(2,1)} %copy.24), calls=%async_computation.2 | async-start | bytes 4194304 | tf_op jit(solution)/shard_map/all_to_all | solution.py:38
  384.6 51.8 %collective-permute-start.13 = (bf16[2,2,64,2048]{3,2,1,0:T(8,128)(2,1)}, bf16[2,2,64,2048]{3,2,1,0:T(8,128)(2,1)}, u32[]{:S(2)}, u32[]{:S(2)}) collective-permute-start(bf16[2,2,64,2048]{3,2,1,0:T(8,128)(2,1)} %collective-permute-done.11), channel_id=1, source_target_pairs={{0,60},{4,0},{8,4},{12,8},{16,12},{20,16},{24,20},{28,24},{32,28},... | collective-permute-start | bytes 3145736 | tf_op jit(solution)/shard_map/ppermute | solution.py:21
  393.9 45.9 %collective-permute-start.14 = (bf16[2,2,64,2048]{3,2,1,0:T(8,128)(2,1)}, bf16[2,2,64,2048]{3,2,1,0:T(8,128)(2,1)}, u32[]{:S(2)}, u32[]{:S(2)}) collective-permute-start(bf16[2,2,64,2048]{3,2,1,0:T(8,128)(2,1)} %collective-permute-done.12), channel_id=1, source_target_pairs={{0,4},{4,8},{8,12},{12,16},{16,20},{20,24},{24,28},{28,32},{32,36}... | collective-permute-start | bytes 3145736 | tf_op jit(solution)/shard_map/ppermute | solution.py:16
  413.7 25.1 %collective-permute-start.16 = (f32[1,2,64,64]{3,2,1,0:T(8,128)S(1)}, f32[1,2,64,64]{3,2,1,0:T(8,128)S(1)}, u32[]{:S(2)}, u32[]{:S(2)}) collective-permute-start(f32[1,2,64,64]{3,2,1,0:T(8,128)S(1)} %psum.30), channel_id=1, source_target_pairs={{0,64},{64,0},{1,65},{65,1},{2,66},{66,2},{3,67},{67,3},{4,68},{68... | collective-permute-start | bytes 98312 | tf_op jit(solution)/shard_map/ppermute | solution.py:30
  448.1 25.8 %collective-permute-start.17 = (bf16[1,2048,512]{2,1,0:T(8,128)(2,1)S(1)}, bf16[1,2048,512]{2,1,0:T(8,128)(2,1)}, u32[]{:S(2)}, u32[]{:S(2)}) collective-permute-start(bf16[1,2048,512]{2,1,0:T(8,128)(2,1)S(1)} %bitcast.71), channel_id=1, source_target_pairs={{0,64},{64,0},{1,65},{65,1},{2,66},{66,2},{3,67},{67,3},{4,68},{68... | collective-permute-start | bytes 6291464 | tf_op jit(solution)/shard_map/ppermute | solution.py:30
  (6 other events, 220.1 us)
Sparse Core Ops, SparseCore 0:
  9.6 51.4 all-gather.3
  149.7 102.3 reduce-scatter.1
  254.2 31.6 all-gather.5
  311.1 44.6 all-reduce.2
